TPU v7x, 512 devices: a whole 4x8x8 slice. The times are simulated.
512 devices in a mesh: dp: 16 (over y, core), ctx: 32 (over z, x).
Axes of the slice: x: 4, y: 8, z: 8, core: 2. Of those that a mesh axis runs over, the one named last changes fastest.
Arguments:
- inner_gate: bfloat16 [65536, 1024], P(('dp', 'ctx')), parts along dimension 0, may hold values from -6 to 6
- outer_gate: bfloat16 [65536, 1024], P(('dp', 'ctx')), parts along dimension 0, may hold values from -6 to 6
- signal: bfloat16 [65536, 1024], P(('dp', 'ctx')), parts along dimension 0, may hold values from -6 to 6
- filters: float32 [64, 128], replicated, may hold values from -0.5 to 0.5
- bypass: float32 [1024], replicated, may hold values from 0.5 to 1.5
- query_rows: bfloat16 [65536, 1024], P(('dp', 'ctx')), parts along dimension 0, may hold values from -25 to 25
- key_rows: bfloat16 [65536, 1024], P(('dp', 'ctx')), parts along dimension 0, may hold values from -4.5 to 4.5
Outputs:
- hyena_out: bfloat16 [65536, 1024], P(('dp', 'ctx')), parts along dimension 0
- attended: bfloat16 [65536, 1024], P(('dp', 'ctx')), parts along dimension 0
There are 16 independent parts, one for each index of `dp`. A program takes and returns all parts, laid end to end along the dimension named above; an argument that names none is the same for every part. Nothing has to cross between parts.
All inputs are finite; a program needn't handle non-finite values.
Results may differ from a plain program's by a relative error of at most 0.006.
Values may be sent and summed in bfloat16 or wider, within the bound.
No kernel may reach another device: no remote copies, remote signals or barrier semaphores. Data moves between devices by JAX's collectives and lax.ppermute only.
A program may use at most 128 MiB of HBM per device.

v0:
```python
import math

import jax
import jax.numpy as jnp
from jax import lax
from jax.sharding import PartitionSpec as P

DH = 128
TAPS = 128


def passed_along(array, axis, by):
    devices = lax.axis_size(axis)
    return lax.ppermute(array, axis, [(i, (i + by) % devices) for i in range(devices)])


def passed_along_2(array, axis, by):
    devices = lax.axis_size(axis)
    pairs = [(i, i + by) for i in range(devices) if 0 <= i + by < devices]
    return lax.ppermute(array, axis, pairs)


def attend(queries, query_pos, key_rows, hyena_out):
    local_rows, channels = queries.shape
    head_count = channels // DH
    query_heads = queries.reshape(local_rows, head_count, DH)
    latest = jnp.max(query_pos)
    inv_root = 1.0 / math.sqrt(DH)

    def update_block(current, key_piece, value_piece, start):
        running_max, running_sum, weighted = current
        piece_rows = key_piece.shape[0]
        key_pos = start + jnp.arange(piece_rows, dtype=jnp.int32)
        key_heads = key_piece.reshape(piece_rows, head_count, DH)
        value_heads = value_piece.reshape(piece_rows, head_count, DH)
        scores = (
            jnp.einsum("thd,phd->thp", query_heads, key_heads, preferred_element_type=jnp.float32)
            * inv_root
        )
        visible = key_pos[None, None, :] <= query_pos[:, None, None]
        scores = jnp.where(visible, scores, -1e30)
        new_max = jnp.maximum(running_max, jnp.max(scores, axis=2))
        weights = jnp.where(visible, jnp.exp(scores - new_max[:, :, None]), 0.0)
        rescale = jnp.exp(running_max - new_max)
        running_sum = running_sum * rescale + jnp.sum(weights, axis=2)
        weighted = weighted * rescale[:, :, None] + jnp.einsum(
            "thp,phd->thd",
            weights.astype(jnp.bfloat16),
            value_heads,
            preferred_element_type=jnp.float32,
        )
        return (new_max, running_sum, weighted)

    def guarded(current, key_piece, value_piece, start):

        def unchanged(state):
            return state

        def changed(state):
            return update_block(state, key_piece, value_piece, start)

        return lax.cond(start > latest, unchanged, changed, current)

    def fold(softmax_state, pieces, start):
        key_piece, value_piece = pieces
        piece_rows = key_piece.shape[0]
        return guarded(softmax_state, key_piece, value_piece, start)

    initial = (
        jnp.full((local_rows, head_count), -1e30, jnp.float32),
        jnp.zeros((local_rows, head_count), jnp.float32),
        jnp.zeros((local_rows, head_count, DH), jnp.float32),
    )
    members = lax.axis_size("ctx")
    my_index = lax.axis_index("ctx")
    block_rows = key_rows.shape[0]
    stacked = jnp.stack([key_rows, hyena_out])
    first_state = fold(initial, (key_rows, hyena_out), my_index * block_rows)

    def chain_step(step_index, carried):
        current, held = carried
        held = passed_along(held, "ctx", 1)
        anchor = (my_index - 1 - step_index) % members
        current = fold(current, (held[0], held[1]), anchor * block_rows)
        return (current, held)

    softmax_state, last_held = lax.fori_loop(0, members - 1, chain_step, (first_state, stacked))
    final_max, final_sum, weighted = softmax_state
    return (weighted / final_sum[:, :, None]).reshape(local_rows, channels).astype(jnp.bfloat16)


def shards(inner_gate, outer_gate, signal, filters, bypass, query_rows, key_rows):
    local_rows, channels = signal.shape
    members = lax.axis_size("ctx")
    my_index = lax.axis_index("ctx")
    product = (inner_gate.astype(jnp.float32) * signal.astype(jnp.float32)).astype(jnp.bfloat16)
    left_rim = passed_along_2(product[local_rows - (TAPS - 1) :], "ctx", 1)
    extended = jnp.concatenate([left_rim, product], axis=0).astype(jnp.float32)
    group_count = filters.shape[0]
    group_width = channels // group_count
    window_rows = 2 * TAPS - 1
    flipped = filters[:, ::-1]
    padded = jnp.concatenate([flipped, jnp.zeros((group_count, TAPS), jnp.float32)], axis=1)
    banded = jnp.tile(padded, (1, TAPS))[:, : TAPS * window_rows].reshape(
        group_count, TAPS, window_rows
    )
    block_count = local_rows // TAPS
    windows = jnp.stack([extended])
    windows = windows.reshape(block_count, window_rows, group_count, group_width)
    convolved = jnp.einsum(
        "gtj,bjgc->btgc", banded, windows, precision=lax.Precision.HIGHEST
    ).reshape(local_rows, channels)
    hyena_out = (
        outer_gate.astype(jnp.float32) * (convolved + bypass[None, :] * product.astype(jnp.float32))
    ).astype(jnp.bfloat16)
    per_source = local_rows // members
    spread = lax.all_to_all(
        query_rows.reshape(per_source, members, channels),
        "ctx",
        split_axis=1,
        concat_axis=1,
        tiled=True,
    )
    source = jnp.arange(members, dtype=jnp.int32)[None, :]
    offset = jnp.arange(per_source, dtype=jnp.int32)[:, None]
    query_pos = (source * local_rows + offset * members + my_index).reshape(local_rows)
    local_queries = spread.reshape(local_rows, channels)
    attended = attend(local_queries, query_pos, key_rows, hyena_out)
    returned = lax.all_to_all(
        attended.reshape(per_source, members, channels),
        "ctx",
        split_axis=1,
        concat_axis=1,
        tiled=True,
    )
    attended = returned.reshape(local_rows, channels)
    return (hyena_out, attended)


def solution(mesh):
    placed = (
        P(("dp", "ctx"), None),
        P(("dp", "ctx"), None),
        P(("dp", "ctx"), None),
        P(),
        P(),
        P(("dp", "ctx"), None),
        P(("dp", "ctx"), None),
    )
    return jax.shard_map(
        shards,
        mesh=mesh,
        in_specs=placed,
        out_specs=(P(("dp", "ctx"), None), P(("dp", "ctx"), None)),
        check_vma=False,
    )
```

profile of v0, /device:TPU:56, one launch (start us, length us, event | category | flops | bytes accessed | tf_op | source)
XLA Modules:
  0.0 632.5 jit_solution(6121067167949745488)
XLA Ops:
  7.1 12.9 %all-to-all-start = ((bf16[4,32,1024]{2,0,1:T(4,128)(2,1)}), bf16[4,32,1024]{2,0,1:T(4,128)(2,1)S(1)}, u32[]{:S(2)}, u32[]{:S(2)}) async-start(bf16[4,32,1024]{2,0,1:T(4,128)(2,1)} %copy.49), calls=%async_computation | async-start | bytes 524288 | tf_op jit(solution)/shard_map/all_to_all | solution.py:117
  30.0 15.9 %reshape.132 = f32[64,128,255]{2,1,0:T(8,128)} reshape(f32[64,32640]{1,0:T(8,128)} %slice.27) | data formatting | bytes 16711680 | tf_op jit(solution)/shard_map/reshape | solution.py:104
  58.6 554.3 %while.22 = (s32[]{:T(128)}, f32[128,8]{0,1:T(8,128)S(1)}, f32[128,8]{0,1:T(8,128)S(1)}, f32[128,8,128]{2,0,1:T(8,128)S(1)}, bf16[2,128,1024]{1,2,0:T(8,128)(2,1...) while((s32[]{:T(128)}, f32[128,8]{0,1:T(8,128)S(1)}, ...), condition=%wide.region_10.11_spmd.clone, body=%wide.region_5.10_spmd.clone.sunk | while | flops 68569488 | bytes 7736928 | solution.py:87
  62.9 14.0 %collective-permute-done = bf16[2,128,1024]{1,2,0:T(8,128)(2,1)S(1)} collective-permute-done((bf16[2,128,1024]{1,2,0:T(8,128)(2,1)S(1)}, bf16[2,128,1024]{1,2,0:T(8,128)(2,1)S(1)}, u32[]{:S(2)}, u32[]{:S(2)}) %collective-permute-start) | collective-permute-done | bytes 524320 | tf_op jit(solution)/shard_map/while/body/eval_jaxpr/ppermute | solution.py:14
  80.8 14.9 %collective-permute-done = bf16[2,128,1024]{1,2,0:T(8,128)(2,1)S(1)} collective-permute-done((bf16[2,128,1024]{1,2,0:T(8,128)(2,1)S(1)}, bf16[2,128,1024]{1,2,0:T(8,128)(2,1)S(1)}, u32[]{:S(2)}, u32[]{:S(2)}) %collective-permute-start) | collective-permute-done | bytes 524320 | tf_op jit(solution)/shard_map/while/body/eval_jaxpr/ppermute | solution.py:14
  99.5 14.0 %collective-permute-done = bf16[2,128,1024]{1,2,0:T(8,128)(2,1)S(1)} collective-permute-done((bf16[2,128,1024]{1,2,0:T(8,128)(2,1)S(1)}, bf16[2,128,1024]{1,2,0:T(8,128)(2,1)S(1)}, u32[]{:S(2)}, u32[]{:S(2)}) %collective-permute-start) | collective-permute-done | bytes 524320 | tf_op jit(solution)/shard_map/while/body/eval_jaxpr/ppermute | solution.py:14
  117.5 13.2 %collective-permute-done = bf16[2,128,1024]{1,2,0:T(8,128)(2,1)S(1)} collective-permute-done((bf16[2,128,1024]{1,2,0:T(8,128)(2,1)S(1)}, bf16[2,128,1024]{1,2,0:T(8,128)(2,1)S(1)}, u32[]{:S(2)}, u32[]{:S(2)}) %collective-permute-start) | collective-permute-done | bytes 524320 | tf_op jit(solution)/shard_map/while/body/eval_jaxpr/ppermute | solution.py:14
  134.5 12.3 %collective-permute-done = bf16[2,128,1024]{1,2,0:T(8,128)(2,1)S(1)} collective-permute-done((bf16[2,128,1024]{1,2,0:T(8,128)(2,1)S(1)}, bf16[2,128,1024]{1,2,0:T(8,128)(2,1)S(1)}, u32[]{:S(2)}, u32[]{:S(2)}) %collective-permute-start) | collective-permute-done | bytes 524320 | tf_op jit(solution)/shard_map/while/body/eval_jaxpr/ppermute | solution.py:14
  150.7 11.8 %collective-permute-done = bf16[2,128,1024]{1,2,0:T(8,128)(2,1)S(1)} collective-permute-done((bf16[2,128,1024]{1,2,0:T(8,128)(2,1)S(1)}, bf16[2,128,1024]{1,2,0:T(8,128)(2,1)S(1)}, u32[]{:S(2)}, u32[]{:S(2)}) %collective-permute-start) | collective-permute-done | bytes 524320 | tf_op jit(solution)/shard_map/while/body/eval_jaxpr/ppermute | solution.py:14
  166.4 11.8 %collective-permute-done = bf16[2,128,1024]{1,2,0:T(8,128)(2,1)S(1)} collective-permute-done((bf16[2,128,1024]{1,2,0:T(8,128)(2,1)S(1)}, bf16[2,128,1024]{1,2,0:T(8,128)(2,1)S(1)}, u32[]{:S(2)}, u32[]{:S(2)}) %collective-permute-start) | collective-permute-done | bytes 524320 | tf_op jit(solution)/shard_map/while/body/eval_jaxpr/ppermute | solution.py:14
  182.1 11.8 %collective-permute-done = bf16[2,128,1024]{1,2,0:T(8,128)(2,1)S(1)} collective-permute-done((bf16[2,128,1024]{1,2,0:T(8,128)(2,1)S(1)}, bf16[2,128,1024]{1,2,0:T(8,128)(2,1)S(1)}, u32[]{:S(2)}, u32[]{:S(2)}) %collective-permute-start) | collective-permute-done | bytes 524320 | tf_op jit(solution)/shard_map/while/body/eval_jaxpr/ppermute | solution.py:14
  197.8 12.3 %collective-permute-done = bf16[2,128,1024]{1,2,0:T(8,128)(2,1)S(1)} collective-permute-done((bf16[2,128,1024]{1,2,0:T(8,128)(2,1)S(1)}, bf16[2,128,1024]{1,2,0:T(8,128)(2,1)S(1)}, u32[]{:S(2)}, u32[]{:S(2)}) %collective-permute-start) | collective-permute-done | bytes 524320 | tf_op jit(solution)/shard_map/while/body/eval_jaxpr/ppermute | solution.py:14
  214.1 13.5 %collective-permute-done = bf16[2,128,1024]{1,2,0:T(8,128)(2,1)S(1)} collective-permute-done((bf16[2,128,1024]{1,2,0:T(8,128)(2,1)S(1)}, bf16[2,128,1024]{1,2,0:T(8,128)(2,1)S(1)}, u32[]{:S(2)}, u32[]{:S(2)}) %collective-permute-start) | collective-permute-done | bytes 524320 | tf_op jit(solution)/shard_map/while/body/eval_jaxpr/ppermute | solution.py:14
  231.4 14.6 %collective-permute-done = bf16[2,128,1024]{1,2,0:T(8,128)(2,1)S(1)} collective-permute-done((bf16[2,128,1024]{1,2,0:T(8,128)(2,1)S(1)}, bf16[2,128,1024]{1,2,0:T(8,128)(2,1)S(1)}, u32[]{:S(2)}, u32[]{:S(2)}) %collective-permute-start) | collective-permute-done | bytes 524320 | tf_op jit(solution)/shard_map/while/body/eval_jaxpr/ppermute | solution.py:14
  249.9 15.8 %collective-permute-done = bf16[2,128,1024]{1,2,0:T(8,128)(2,1)S(1)} collective-permute-done((bf16[2,128,1024]{1,2,0:T(8,128)(2,1)S(1)}, bf16[2,128,1024]{1,2,0:T(8,128)(2,1)S(1)}, u32[]{:S(2)}, u32[]{:S(2)}) %collective-permute-start) | collective-permute-done | bytes 524320 | tf_op jit(solution)/shard_map/while/body/eval_jaxpr/ppermute | solution.py:14
  269.6 16.9 %collective-permute-done = bf16[2,128,1024]{1,2,0:T(8,128)(2,1)S(1)} collective-permute-done((bf16[2,128,1024]{1,2,0:T(8,128)(2,1)S(1)}, bf16[2,128,1024]{1,2,0:T(8,128)(2,1)S(1)}, u32[]{:S(2)}, u32[]{:S(2)}) %collective-permute-start) | collective-permute-done | bytes 524320 | tf_op jit(solution)/shard_map/while/body/eval_jaxpr/ppermute | solution.py:14
  290.4 16.8 %collective-permute-done = bf16[2,128,1024]{1,2,0:T(8,128)(2,1)S(1)} collective-permute-done((bf16[2,128,1024]{1,2,0:T(8,128)(2,1)S(1)}, bf16[2,128,1024]{1,2,0:T(8,128)(2,1)S(1)}, u32[]{:S(2)}, u32[]{:S(2)}) %collective-permute-start) | collective-permute-done | bytes 524320 | tf_op jit(solution)/shard_map/while/body/eval_jaxpr/ppermute | solution.py:14
  311.1 16.0 %collective-permute-done = bf16[2,128,1024]{1,2,0:T(8,128)(2,1)S(1)} collective-permute-done((bf16[2,128,1024]{1,2,0:T(8,128)(2,1)S(1)}, bf16[2,128,1024]{1,2,0:T(8,128)(2,1)S(1)}, u32[]{:S(2)}, u32[]{:S(2)}) %collective-permute-start) | collective-permute-done | bytes 524320 | tf_op jit(solution)/shard_map/while/body/eval_jaxpr/ppermute | solution.py:14
  330.9 15.1 %collective-permute-done = bf16[2,128,1024]{1,2,0:T(8,128)(2,1)S(1)} collective-permute-done((bf16[2,128,1024]{1,2,0:T(8,128)(2,1)S(1)}, bf16[2,128,1024]{1,2,0:T(8,128)(2,1)S(1)}, u32[]{:S(2)}, u32[]{:S(2)}) %collective-permute-start) | collective-permute-done | bytes 524320 | tf_op jit(solution)/shard_map/while/body/eval_jaxpr/ppermute | solution.py:14
  349.9 14.3 %collective-permute-done = bf16[2,128,1024]{1,2,0:T(8,128)(2,1)S(1)} collective-permute-done((bf16[2,128,1024]{1,2,0:T(8,128)(2,1)S(1)}, bf16[2,128,1024]{1,2,0:T(8,128)(2,1)S(1)}, u32[]{:S(2)}, u32[]{:S(2)}) %collective-permute-start) | collective-permute-done | bytes 524320 | tf_op jit(solution)/shard_map/while/body/eval_jaxpr/ppermute | solution.py:14
  368.1 13.4 %collective-permute-done = bf16[2,128,1024]{1,2,0:T(8,128)(2,1)S(1)} collective-permute-done((bf16[2,128,1024]{1,2,0:T(8,128)(2,1)S(1)}, bf16[2,128,1024]{1,2,0:T(8,128)(2,1)S(1)}, u32[]{:S(2)}, u32[]{:S(2)}) %collective-permute-start) | collective-permute-done | bytes 524320 | tf_op jit(solution)/shard_map/while/body/eval_jaxpr/ppermute | solution.py:14
  385.4 12.5 %collective-permute-done = bf16[2,128,1024]{1,2,0:T(8,128)(2,1)S(1)} collective-permute-done((bf16[2,128,1024]{1,2,0:T(8,128)(2,1)S(1)}, bf16[2,128,1024]{1,2,0:T(8,128)(2,1)S(1)}, u32[]{:S(2)}, u32[]{:S(2)}) %collective-permute-start) | collective-permute-done | bytes 524320 | tf_op jit(solution)/shard_map/while/body/eval_jaxpr/ppermute | solution.py:14
  401.8 11.8 %collective-permute-done = bf16[2,128,1024]{1,2,0:T(8,128)(2,1)S(1)} collective-permute-done((bf16[2,128,1024]{1,2,0:T(8,128)(2,1)S(1)}, bf16[2,128,1024]{1,2,0:T(8,128)(2,1)S(1)}, u32[]{:S(2)}, u32[]{:S(2)}) %collective-permute-start) | collective-permute-done | bytes 524320 | tf_op jit(solution)/shard_map/while/body/eval_jaxpr/ppermute | solution.py:14
  449.0 12.1 %collective-permute-done = bf16[2,128,1024]{1,2,0:T(8,128)(2,1)S(1)} collective-permute-done((bf16[2,128,1024]{1,2,0:T(8,128)(2,1)S(1)}, bf16[2,128,1024]{1,2,0:T(8,128)(2,1)S(1)}, u32[]{:S(2)}, u32[]{:S(2)}) %collective-permute-start) | collective-permute-done | bytes 524320 | tf_op jit(solution)/shard_map/while/body/eval_jaxpr/ppermute | solution.py:14
  464.9 13.2 %collective-permute-done = bf16[2,128,1024]{1,2,0:T(8,128)(2,1)S(1)} collective-permute-done((bf16[2,128,1024]{1,2,0:T(8,128)(2,1)S(1)}, bf16[2,128,1024]{1,2,0:T(8,128)(2,1)S(1)}, u32[]{:S(2)}, u32[]{:S(2)}) %collective-permute-start) | collective-permute-done | bytes 524320 | tf_op jit(solution)/shard_map/while/body/eval_jaxpr/ppermute | solution.py:14
  482.1 14.4 %collective-permute-done = bf16[2,128,1024]{1,2,0:T(8,128)(2,1)S(1)} collective-permute-done((bf16[2,128,1024]{1,2,0:T(8,128)(2,1)S(1)}, bf16[2,128,1024]{1,2,0:T(8,128)(2,1)S(1)}, u32[]{:S(2)}, u32[]{:S(2)}) %collective-permute-start) | collective-permute-done | bytes 524320 | tf_op jit(solution)/shard_map/while/body/eval_jaxpr/ppermute | solution.py:14
  500.4 15.5 %collective-permute-done = bf16[2,128,1024]{1,2,0:T(8,128)(2,1)S(1)} collective-permute-done((bf16[2,128,1024]{1,2,0:T(8,128)(2,1)S(1)}, bf16[2,128,1024]{1,2,0:T(8,128)(2,1)S(1)}, u32[]{:S(2)}, u32[]{:S(2)}) %collective-permute-start) | collective-permute-done | bytes 524320 | tf_op jit(solution)/shard_map/while/body/eval_jaxpr/ppermute | solution.py:14
  519.8 16.7 %collective-permute-done = bf16[2,128,1024]{1,2,0:T(8,128)(2,1)S(1)} collective-permute-done((bf16[2,128,1024]{1,2,0:T(8,128)(2,1)S(1)}, bf16[2,128,1024]{1,2,0:T(8,128)(2,1)S(1)}, u32[]{:S(2)}, u32[]{:S(2)}) %collective-permute-start) | collective-permute-done | bytes 524320 | tf_op jit(solution)/shard_map/while/body/eval_jaxpr/ppermute | solution.py:14
  540.4 17.0 %collective-permute-done = bf16[2,128,1024]{1,2,0:T(8,128)(2,1)S(1)} collective-permute-done((bf16[2,128,1024]{1,2,0:T(8,128)(2,1)S(1)}, bf16[2,128,1024]{1,2,0:T(8,128)(2,1)S(1)}, u32[]{:S(2)}, u32[]{:S(2)}) %collective-permute-start) | collective-permute-done | bytes 524320 | tf_op jit(solution)/shard_map/while/body/eval_jaxpr/ppermute | solution.py:14
  561.3 16.2 %collective-permute-done = bf16[2,128,1024]{1,2,0:T(8,128)(2,1)S(1)} collective-permute-done((bf16[2,128,1024]{1,2,0:T(8,128)(2,1)S(1)}, bf16[2,128,1024]{1,2,0:T(8,128)(2,1)S(1)}, u32[]{:S(2)}, u32[]{:S(2)}) %collective-permute-start) | collective-permute-done | bytes 524320 | tf_op jit(solution)/shard_map/while/body/eval_jaxpr/ppermute | solution.py:14
  581.4 14.5 %collective-permute-done = bf16[2,128,1024]{1,2,0:T(8,128)(2,1)S(1)} collective-permute-done((bf16[2,128,1024]{1,2,0:T(8,128)(2,1)S(1)}, bf16[2,128,1024]{1,2,0:T(8,128)(2,1)S(1)}, u32[]{:S(2)}, u32[]{:S(2)}) %collective-permute-start) | collective-permute-done | bytes 524320 | tf_op jit(solution)/shard_map/while/body/eval_jaxpr/ppermute | solution.py:14
  613.6 18.1 %all_to_all.10 = bf16[4,32,1024]{2,0,1:T(4,128)(2,1)S(1)} all-to-all(bf16[4,32,1024]{2,0,1:T(4,128)(2,1)S(1)} %copy.55), channel_id=1, replica_groups=mesh['dp'=16,'ctx'=32] {'ctx'}, dimensions={1} | all-to-all | bytes 524288 | tf_op jit(solution)/shard_map/all_to_all | solution.py:129
  (481 shorter events, 205.1 us)
Async XLA Ops:
  1.8 45.5 %collective-permute-start.1 = (bf16[127,1024]{1,0:T(8,128)(2,1)S(1)}, bf16[127,1024]{1,0:T(8,128)(2,1)S(1)}, u32[]{:S(2)}, u32[]{:S(2)}) collective-permute-start(bf16[127,1024]{1,0:T(8,128)(2,1)S(1)} %slice.26), channel_id=1, source_target_pairs={{0,1},{1,2},{2,3},{3,4},{4,5},{5,6},{6,7},{7,8},{8,9},{9,10},{10,1... | collective-permute-start | bytes 780296 | tf_op jit(solution)/shard_map/ppermute | solution.py:20
  7.1 49.2 %all-to-all-start = ((bf16[4,32,1024]{2,0,1:T(4,128)(2,1)}), bf16[4,32,1024]{2,0,1:T(4,128)(2,1)S(1)}, u32[]{:S(2)}, u32[]{:S(2)}) async-start(bf16[4,32,1024]{2,0,1:T(4,128)(2,1)} %copy.49), calls=%async_computation | async-start | bytes 524288 | tf_op jit(solution)/shard_map/all_to_all | solution.py:117
  58.6 18.3 %collective-permute-start = (bf16[2,128,1024]{1,2,0:T(8,128)(2,1)S(1)}, bf16[2,128,1024]{1,2,0:T(8,128)(2,1)S(1)}, u32[]{:S(2)}, u32[]{:S(2)}) collective-permute-start(bf16[2,128,1024]{1,2,0:T(8,128)(2,1)S(1)} %get-tuple-element.522), channel_id=1, source_target_pairs={{0,1},{1,2},{2,3},{3,4},{4,5},{5,6},{6,7},{7,8},{8,9},{9,10},{10,1... | collective-permute-start | bytes 1572872 | tf_op jit(solution)/shard_map/while/body/eval_jaxpr/ppermute | solution.py:14
  78.2 17.4 %collective-permute-start = (bf16[2,128,1024]{1,2,0:T(8,128)(2,1)S(1)}, bf16[2,128,1024]{1,2,0:T(8,128)(2,1)S(1)}, u32[]{:S(2)}, u32[]{:S(2)}) collective-permute-start(bf16[2,128,1024]{1,2,0:T(8,128)(2,1)S(1)} %get-tuple-element.522), channel_id=1, source_target_pairs={{0,1},{1,2},{2,3},{3,4},{4,5},{5,6},{6,7},{7,8},{8,9},{9,10},{10,1... | collective-permute-start | bytes 1572872 | tf_op jit(solution)/shard_map/while/body/eval_jaxpr/ppermute | solution.py:14
  97.0 16.6 %collective-permute-start = (bf16[2,128,1024]{1,2,0:T(8,128)(2,1)S(1)}, bf16[2,128,1024]{1,2,0:T(8,128)(2,1)S(1)}, u32[]{:S(2)}, u32[]{:S(2)}) collective-permute-start(bf16[2,128,1024]{1,2,0:T(8,128)(2,1)S(1)} %get-tuple-element.522), channel_id=1, source_target_pairs={{0,1},{1,2},{2,3},{3,4},{4,5},{5,6},{6,7},{7,8},{8,9},{9,10},{10,1... | collective-permute-start | bytes 1572872 | tf_op jit(solution)/shard_map/while/body/eval_jaxpr/ppermute | solution.py:14
  114.9 15.7 %collective-permute-start = (bf16[2,128,1024]{1,2,0:T(8,128)(2,1)S(1)}, bf16[2,128,1024]{1,2,0:T(8,128)(2,1)S(1)}, u32[]{:S(2)}, u32[]{:S(2)}) collective-permute-start(bf16[2,128,1024]{1,2,0:T(8,128)(2,1)S(1)} %get-tuple-element.522), channel_id=1, source_target_pairs={{0,1},{1,2},{2,3},{3,4},{4,5},{5,6},{6,7},{7,8},{8,9},{9,10},{10,1... | collective-permute-start | bytes 1572872 | tf_op jit(solution)/shard_map/while/body/eval_jaxpr/ppermute | solution.py:14
  131.9 14.9 %collective-permute-start = (bf16[2,128,1024]{1,2,0:T(8,128)(2,1)S(1)}, bf16[2,128,1024]{1,2,0:T(8,128)(2,1)S(1)}, u32[]{:S(2)}, u32[]{:S(2)}) collective-permute-start(bf16[2,128,1024]{1,2,0:T(8,128)(2,1)S(1)} %get-tuple-element.522), channel_id=1, source_target_pairs={{0,1},{1,2},{2,3},{3,4},{4,5},{5,6},{6,7},{7,8},{8,9},{9,10},{10,1... | collective-permute-start | bytes 1572872 | tf_op jit(solution)/shard_map/while/body/eval_jaxpr/ppermute | solution.py:14
  148.1 14.4 %collective-permute-start = (bf16[2,128,1024]{1,2,0:T(8,128)(2,1)S(1)}, bf16[2,128,1024]{1,2,0:T(8,128)(2,1)S(1)}, u32[]{:S(2)}, u32[]{:S(2)}) collective-permute-start(bf16[2,128,1024]{1,2,0:T(8,128)(2,1)S(1)} %get-tuple-element.522), channel_id=1, source_target_pairs={{0,1},{1,2},{2,3},{3,4},{4,5},{5,6},{6,7},{7,8},{8,9},{9,10},{10,1... | collective-permute-start | bytes 1572872 | tf_op jit(solution)/shard_map/while/body/eval_jaxpr/ppermute | solution.py:14
  163.8 14.4 %collective-permute-start = (bf16[2,128,1024]{1,2,0:T(8,128)(2,1)S(1)}, bf16[2,128,1024]{1,2,0:T(8,128)(2,1)S(1)}, u32[]{:S(2)}, u32[]{:S(2)}) collective-permute-start(bf16[2,128,1024]{1,2,0:T(8,128)(2,1)S(1)} %get-tuple-element.522), channel_id=1, source_target_pairs={{0,1},{1,2},{2,3},{3,4},{4,5},{5,6},{6,7},{7,8},{8,9},{9,10},{10,1... | collective-permute-start | bytes 1572872 | tf_op jit(solution)/shard_map/while/body/eval_jaxpr/ppermute | solution.py:14
  179.6 14.4 %collective-permute-start = (bf16[2,128,1024]{1,2,0:T(8,128)(2,1)S(1)}, bf16[2,128,1024]{1,2,0:T(8,128)(2,1)S(1)}, u32[]{:S(2)}, u32[]{:S(2)}) collective-permute-start(bf16[2,128,1024]{1,2,0:T(8,128)(2,1)S(1)} %get-tuple-element.522), channel_id=1, source_target_pairs={{0,1},{1,2},{2,3},{3,4},{4,5},{5,6},{6,7},{7,8},{8,9},{9,10},{10,1... | collective-permute-start | bytes 1572872 | tf_op jit(solution)/shard_map/while/body/eval_jaxpr/ppermute | solution.py:14
  195.3 14.9 %collective-permute-start = (bf16[2,128,1024]{1,2,0:T(8,128)(2,1)S(1)}, bf16[2,128,1024]{1,2,0:T(8,128)(2,1)S(1)}, u32[]{:S(2)}, u32[]{:S(2)}) collective-permute-start(bf16[2,128,1024]{1,2,0:T(8,128)(2,1)S(1)} %get-tuple-element.522), channel_id=1, source_target_pairs={{0,1},{1,2},{2,3},{3,4},{4,5},{5,6},{6,7},{7,8},{8,9},{9,10},{10,1... | collective-permute-start | bytes 1572872 | tf_op jit(solution)/shard_map/while/body/eval_jaxpr/ppermute | solution.py:14
  211.5 16.0 %collective-permute-start = (bf16[2,128,1024]{1,2,0:T(8,128)(2,1)S(1)}, bf16[2,128,1024]{1,2,0:T(8,128)(2,1)S(1)}, u32[]{:S(2)}, u32[]{:S(2)}) collective-permute-start(bf16[2,128,1024]{1,2,0:T(8,128)(2,1)S(1)} %get-tuple-element.522), channel_id=1, source_target_pairs={{0,1},{1,2},{2,3},{3,4},{4,5},{5,6},{6,7},{7,8},{8,9},{9,10},{10,1... | collective-permute-start | bytes 1572872 | tf_op jit(solution)/shard_map/while/body/eval_jaxpr/ppermute | solution.py:14
  228.8 17.2 %collective-permute-start = (bf16[2,128,1024]{1,2,0:T(8,128)(2,1)S(1)}, bf16[2,128,1024]{1,2,0:T(8,128)(2,1)S(1)}, u32[]{:S(2)}, u32[]{:S(2)}) collective-permute-start(bf16[2,128,1024]{1,2,0:T(8,128)(2,1)S(1)} %get-tuple-element.522), channel_id=1, source_target_pairs={{0,1},{1,2},{2,3},{3,4},{4,5},{5,6},{6,7},{7,8},{8,9},{9,10},{10,1... | collective-permute-start | bytes 1572872 | tf_op jit(solution)/shard_map/while/body/eval_jaxpr/ppermute | solution.py:14
  247.3 18.3 %collective-permute-start = (bf16[2,128,1024]{1,2,0:T(8,128)(2,1)S(1)}, bf16[2,128,1024]{1,2,0:T(8,128)(2,1)S(1)}, u32[]{:S(2)}, u32[]{:S(2)}) collective-permute-start(bf16[2,128,1024]{1,2,0:T(8,128)(2,1)S(1)} %get-tuple-element.522), channel_id=1, source_target_pairs={{0,1},{1,2},{2,3},{3,4},{4,5},{5,6},{6,7},{7,8},{8,9},{9,10},{10,1... | collective-permute-start | bytes 1572872 | tf_op jit(solution)/shard_map/while/body/eval_jaxpr/ppermute | solution.py:14
  267.0 19.5 %collective-permute-start = (bf16[2,128,1024]{1,2,0:T(8,128)(2,1)S(1)}, bf16[2,128,1024]{1,2,0:T(8,128)(2,1)S(1)}, u32[]{:S(2)}, u32[]{:S(2)}) collective-permute-start(bf16[2,128,1024]{1,2,0:T(8,128)(2,1)S(1)} %get-tuple-element.522), channel_id=1, source_target_pairs={{0,1},{1,2},{2,3},{3,4},{4,5},{5,6},{6,7},{7,8},{8,9},{9,10},{10,1... | collective-permute-start | bytes 1572872 | tf_op jit(solution)/shard_map/while/body/eval_jaxpr/ppermute | solution.py:14
  287.8 19.4 %collective-permute-start = (bf16[2,128,1024]{1,2,0:T(8,128)(2,1)S(1)}, bf16[2,128,1024]{1,2,0:T(8,128)(2,1)S(1)}, u32[]{:S(2)}, u32[]{:S(2)}) collective-permute-start(bf16[2,128,1024]{1,2,0:T(8,128)(2,1)S(1)} %get-tuple-element.522), channel_id=1, source_target_pairs={{0,1},{1,2},{2,3},{3,4},{4,5},{5,6},{6,7},{7,8},{8,9},{9,10},{10,1... | collective-permute-start | bytes 1572872 | tf_op jit(solution)/shard_map/while/body/eval_jaxpr/ppermute | solution.py:14
  308.5 18.5 %collective-permute-start = (bf16[2,128,1024]{1,2,0:T(8,128)(2,1)S(1)}, bf16[2,128,1024]{1,2,0:T(8,128)(2,1)S(1)}, u32[]{:S(2)}, u32[]{:S(2)}) collective-permute-start(bf16[2,128,1024]{1,2,0:T(8,128)(2,1)S(1)} %get-tuple-element.522), channel_id=1, source_target_pairs={{0,1},{1,2},{2,3},{3,4},{4,5},{5,6},{6,7},{7,8},{8,9},{9,10},{10,1... | collective-permute-start | bytes 1572872 | tf_op jit(solution)/shard_map/while/body/eval_jaxpr/ppermute | solution.py:14
  328.4 17.7 %collective-permute-start = (bf16[2,128,1024]{1,2,0:T(8,128)(2,1)S(1)}, bf16[2,128,1024]{1,2,0:T(8,128)(2,1)S(1)}, u32[]{:S(2)}, u32[]{:S(2)}) collective-permute-start(bf16[2,128,1024]{1,2,0:T(8,128)(2,1)S(1)} %get-tuple-element.522), channel_id=1, source_target_pairs={{0,1},{1,2},{2,3},{3,4},{4,5},{5,6},{6,7},{7,8},{8,9},{9,10},{10,1... | collective-permute-start | bytes 1572872 | tf_op jit(solution)/shard_map/while/body/eval_jaxpr/ppermute | solution.py:14
  347.4 16.8 %collective-permute-start = (bf16[2,128,1024]{1,2,0:T(8,128)(2,1)S(1)}, bf16[2,128,1024]{1,2,0:T(8,128)(2,1)S(1)}, u32[]{:S(2)}, u32[]{:S(2)}) collective-permute-start(bf16[2,128,1024]{1,2,0:T(8,128)(2,1)S(1)} %get-tuple-element.522), channel_id=1, source_target_pairs={{0,1},{1,2},{2,3},{3,4},{4,5},{5,6},{6,7},{7,8},{8,9},{9,10},{10,1... | collective-permute-start | bytes 1572872 | tf_op jit(solution)/shard_map/while/body/eval_jaxpr/ppermute | solution.py:14
  365.5 16.0 %collective-permute-start = (bf16[2,128,1024]{1,2,0:T(8,128)(2,1)S(1)}, bf16[2,128,1024]{1,2,0:T(8,128)(2,1)S(1)}, u32[]{:S(2)}, u32[]{:S(2)}) collective-permute-start(bf16[2,128,1024]{1,2,0:T(8,128)(2,1)S(1)} %get-tuple-element.522), channel_id=1, source_target_pairs={{0,1},{1,2},{2,3},{3,4},{4,5},{5,6},{6,7},{7,8},{8,9},{9,10},{10,1... | collective-permute-start | bytes 1572872 | tf_op jit(solution)/shard_map/while/body/eval_jaxpr/ppermute | solution.py:14
  382.8 15.1 %collective-permute-start = (bf16[2,128,1024]{1,2,0:T(8,128)(2,1)S(1)}, bf16[2,128,1024]{1,2,0:T(8,128)(2,1)S(1)}, u32[]{:S(2)}, u32[]{:S(2)}) collective-permute-start(bf16[2,128,1024]{1,2,0:T(8,128)(2,1)S(1)} %get-tuple-element.522), channel_id=1, source_target_pairs={{0,1},{1,2},{2,3},{3,4},{4,5},{5,6},{6,7},{7,8},{8,9},{9,10},{10,1... | collective-permute-start | bytes 1572872 | tf_op jit(solution)/shard_map/while/body/eval_jaxpr/ppermute | solution.py:14
  399.2 14.4 %collective-permute-start = (bf16[2,128,1024]{1,2,0:T(8,128)(2,1)S(1)}, bf16[2,128,1024]{1,2,0:T(8,128)(2,1)S(1)}, u32[]{:S(2)}, u32[]{:S(2)}) collective-permute-start(bf16[2,128,1024]{1,2,0:T(8,128)(2,1)S(1)} %get-tuple-element.522), channel_id=1, source_target_pairs={{0,1},{1,2},{2,3},{3,4},{4,5},{5,6},{6,7},{7,8},{8,9},{9,10},{10,1... | collective-permute-start | bytes 1572872 | tf_op jit(solution)/shard_map/while/body/eval_jaxpr/ppermute | solution.py:14
  415.0 14.4 %collective-permute-start = (bf16[2,128,1024]{1,2,0:T(8,128)(2,1)S(1)}, bf16[2,128,1024]{1,2,0:T(8,128)(2,1)S(1)}, u32[]{:S(2)}, u32[]{:S(2)}) collective-permute-start(bf16[2,128,1024]{1,2,0:T(8,128)(2,1)S(1)} %get-tuple-element.522), channel_id=1, source_target_pairs={{0,1},{1,2},{2,3},{3,4},{4,5},{5,6},{6,7},{7,8},{8,9},{9,10},{10,1... | collective-permute-start | bytes 1572872 | tf_op jit(solution)/shard_map/while/body/eval_jaxpr/ppermute | solution.py:14
  430.7 14.4 %collective-permute-start = (bf16[2,128,1024]{1,2,0:T(8,128)(2,1)S(1)}, bf16[2,128,1024]{1,2,0:T(8,128)(2,1)S(1)}, u32[]{:S(2)}, u32[]{:S(2)}) collective-permute-start(bf16[2,128,1024]{1,2,0:T(8,128)(2,1)S(1)} %get-tuple-element.522), channel_id=1, source_target_pairs={{0,1},{1,2},{2,3},{3,4},{4,5},{5,6},{6,7},{7,8},{8,9},{9,10},{10,1... | collective-permute-start | bytes 1572872 | tf_op jit(solution)/shard_map/while/body/eval_jaxpr/ppermute | solution.py:14
  446.4 14.7 %collective-permute-start = (bf16[2,128,1024]{1,2,0:T(8,128)(2,1)S(1)}, bf16[2,128,1024]{1,2,0:T(8,128)(2,1)S(1)}, u32[]{:S(2)}, u32[]{:S(2)}) collective-permute-start(bf16[2,128,1024]{1,2,0:T(8,128)(2,1)S(1)} %get-tuple-element.522), channel_id=1, source_target_pairs={{0,1},{1,2},{2,3},{3,4},{4,5},{5,6},{6,7},{7,8},{8,9},{9,10},{10,1... | collective-permute-start | bytes 1572872 | tf_op jit(solution)/shard_map/while/body/eval_jaxpr/ppermute | solution.py:14
  462.4 15.8 %collective-permute-start = (bf16[2,128,1024]{1,2,0:T(8,128)(2,1)S(1)}, bf16[2,128,1024]{1,2,0:T(8,128)(2,1)S(1)}, u32[]{:S(2)}, u32[]{:S(2)}) collective-permute-start(bf16[2,128,1024]{1,2,0:T(8,128)(2,1)S(1)} %get-tuple-element.522), channel_id=1, source_target_pairs={{0,1},{1,2},{2,3},{3,4},{4,5},{5,6},{6,7},{7,8},{8,9},{9,10},{10,1... | collective-permute-start | bytes 1572872 | tf_op jit(solution)/shard_map/while/body/eval_jaxpr/ppermute | solution.py:14
  479.5 17.0 %collective-permute-start = (bf16[2,128,1024]{1,2,0:T(8,128)(2,1)S(1)}, bf16[2,128,1024]{1,2,0:T(8,128)(2,1)S(1)}, u32[]{:S(2)}, u32[]{:S(2)}) collective-permute-start(bf16[2,128,1024]{1,2,0:T(8,128)(2,1)S(1)} %get-tuple-element.522), channel_id=1, source_target_pairs={{0,1},{1,2},{2,3},{3,4},{4,5},{5,6},{6,7},{7,8},{8,9},{9,10},{10,1... | collective-permute-start | bytes 1572872 | tf_op jit(solution)/shard_map/while/body/eval_jaxpr/ppermute | solution.py:14
  497.8 18.1 %collective-permute-start = (bf16[2,128,1024]{1,2,0:T(8,128)(2,1)S(1)}, bf16[2,128,1024]{1,2,0:T(8,128)(2,1)S(1)}, u32[]{:S(2)}, u32[]{:S(2)}) collective-permute-start(bf16[2,128,1024]{1,2,0:T(8,128)(2,1)S(1)} %get-tuple-element.522), channel_id=1, source_target_pairs={{0,1},{1,2},{2,3},{3,4},{4,5},{5,6},{6,7},{7,8},{8,9},{9,10},{10,1... | collective-permute-start | bytes 1572872 | tf_op jit(solution)/shard_map/while/body/eval_jaxpr/ppermute | solution.py:14
  517.2 19.3 %collective-permute-start = (bf16[2,128,1024]{1,2,0:T(8,128)(2,1)S(1)}, bf16[2,128,1024]{1,2,0:T(8,128)(2,1)S(1)}, u32[]{:S(2)}, u32[]{:S(2)}) collective-permute-start(bf16[2,128,1024]{1,2,0:T(8,128)(2,1)S(1)} %get-tuple-element.522), channel_id=1, source_target_pairs={{0,1},{1,2},{2,3},{3,4},{4,5},{5,6},{6,7},{7,8},{8,9},{9,10},{10,1... | collective-permute-start | bytes 1572872 | tf_op jit(solution)/shard_map/while/body/eval_jaxpr/ppermute | solution.py:14
  537.8 19.6 %collective-permute-start = (bf16[2,128,1024]{1,2,0:T(8,128)(2,1)S(1)}, bf16[2,128,1024]{1,2,0:T(8,128)(2,1)S(1)}, u32[]{:S(2)}, u32[]{:S(2)}) collective-permute-start(bf16[2,128,1024]{1,2,0:T(8,128)(2,1)S(1)} %get-tuple-element.522), channel_id=1, source_target_pairs={{0,1},{1,2},{2,3},{3,4},{4,5},{5,6},{6,7},{7,8},{8,9},{9,10},{10,1... | collective-permute-start | bytes 1572872 | tf_op jit(solution)/shard_map/while/body/eval_jaxpr/ppermute | solution.py:14
  558.7 18.8 %collective-permute-start = (bf16[2,128,1024]{1,2,0:T(8,128)(2,1)S(1)}, bf16[2,128,1024]{1,2,0:T(8,128)(2,1)S(1)}, u32[]{:S(2)}, u32[]{:S(2)}) collective-permute-start(bf16[2,128,1024]{1,2,0:T(8,128)(2,1)S(1)} %get-tuple-element.522), channel_id=1, source_target_pairs={{0,1},{1,2},{2,3},{3,4},{4,5},{5,6},{6,7},{7,8},{8,9},{9,10},{10,1... | collective-permute-start | bytes 1572872 | tf_op jit(solution)/shard_map/while/body/eval_jaxpr/ppermute | solution.py:14
  578.8 17.0 %collective-permute-start = (bf16[2,128,1024]{1,2,0:T(8,128)(2,1)S(1)}, bf16[2,128,1024]{1,2,0:T(8,128)(2,1)S(1)}, u32[]{:S(2)}, u32[]{:S(2)}) collective-permute-start(bf16[2,128,1024]{1,2,0:T(8,128)(2,1)S(1)} %get-tuple-element.522), channel_id=1, source_target_pairs={{0,1},{1,2},{2,3},{3,4},{4,5},{5,6},{6,7},{7,8},{8,9},{9,10},{10,1... | collective-permute-start | bytes 1572872 | tf_op jit(solution)/shard_map/while/body/eval_jaxpr/ppermute | solution.py:14
  (4 other events, 39.9 us)
where the time goes:
time: 634 us; the launch traced here: 632 us
  waiting for transfers between devices  432 us (68%)
  starting transfers between devices  77.6 us (12%)
  local copies, waits for them, and re-layouts  35 us (6%)
  matrix products  32.3 us (5%)
  loops' own time  23.1 us (4%)
  blocking collectives  18.1 us (3%)
  other arithmetic  13 us (2%)
    ppermute x31, waiting for transfers between devices, passed_along(): lax.ppermute(array, axis, [(i, (i + by) % devices) for i in range(devices)])  432 us
    ppermute x31, starting transfers between devices, passed_along(): lax.ppermute(array, axis, [(i, (i + by) % devices) for i in range(devices)])  61.3 us
    another operation x1, loops' own time, attend(): lax.fori_loop(0, members - 1, chain_step, (first_state, stacked))  21.4 us
    all_to_all x1, blocking collectives, shards(): lax.all_to_all(attended.reshape(per_source, members, channels), 'ctx', sp...  18.1 us
    reshape x1, local copies, waits for them, and re-layouts, shards(): jnp.tile(padded, (1, TAPS))[:, :TAPS * window_rows]  15.9 us
    dot_general x32, matrix products, update_block(): jnp.einsum('thp,phd->thd', weights.astype(jnp.bfloat16), value_heads, pre...  15 us
    all_to_all x1, starting transfers between devices, shards(): lax.all_to_all(query_rows.reshape(per_source, members, channels), 'ctx',...  12.9 us
  transfers between devices with their start and end apart: 33, of which 31 were waited for; matrix products, arithmetic and copies ran while one was open for 6% of the time, Pallas kernels for 0%

commit v1 on v0

v1 whole, which is shorter than its diff:
```python
import math

import numpy as np
import jax
import jax.numpy as jnp
from jax import lax
from jax.sharding import Mesh, PartitionSpec as P
from jax.experimental import pallas as pl
from jax.experimental.pallas import tpu as pltpu

DH = 128
TAPS = 128


def banded_halves(filters, window_rows):
    group_count, taps = filters.shape
    flipped = filters[:, ::-1]
    padded = jnp.concatenate([flipped, jnp.zeros((group_count, taps), jnp.float32)], axis=1)
    hi = padded.astype(jnp.bfloat16)
    lo = (padded - hi.astype(jnp.float32)).astype(jnp.bfloat16)

    def band(half):
        return jnp.tile(half, (1, taps))[:, : taps * window_rows].reshape(
            group_count, taps, window_rows
        )

    return band(hi), band(lo)


def attend_kernel(x_ref, q_ref, k_ref, v_ref, o_ref, *, nx):
    x = x_ref[0]
    blocks, rows, _ = q_ref.shape
    inv_root = 1.0 / math.sqrt(DH)
    for i in range(blocks):
        length = (i + 1) * nx * rows
        q = q_ref[i]
        k = k_ref[:length, :]
        s = lax.dot_general(
            q, k, (((1,), (1,)), ((), ())), preferred_element_type=jnp.float32
        ) * inv_root
        qpos = (i * nx + x) * rows + lax.broadcasted_iota(jnp.int32, (rows, length), 0)
        kpos = lax.broadcasted_iota(jnp.int32, (rows, length), 1)
        visible = kpos <= qpos
        s = jnp.where(visible, s, -1e30)
        highest = jnp.max(s, axis=1, keepdims=True)
        w = jnp.where(visible, jnp.exp(s - highest), 0.0)
        total = jnp.sum(w, axis=1, keepdims=True)
        o = jnp.dot(w.astype(jnp.bfloat16), v_ref[:length, :], preferred_element_type=jnp.float32)
        o_ref[i] = (o / total).astype(o_ref.dtype)


def attend_local(x_index, q, k, v, nx):
    blocks, rows, dh = q.shape
    seq = k.shape[0]
    flops = 2 * 2 * blocks * rows * seq * dh // 2
    return pl.pallas_call(
        lambda *refs: attend_kernel(*refs, nx=nx),
        out_shape=jax.ShapeDtypeStruct(q.shape, jnp.bfloat16),
        in_specs=[
            pl.BlockSpec(memory_space=pltpu.SMEM),
            pl.BlockSpec(memory_space=pltpu.VMEM),
            pl.BlockSpec(memory_space=pltpu.VMEM),
            pl.BlockSpec(memory_space=pltpu.VMEM),
        ],
        out_specs=pl.BlockSpec(memory_space=pltpu.VMEM),
        compiler_params=pltpu.CompilerParams(vmem_limit_bytes=48 * 1024 * 1024),
        cost_estimate=pl.CostEstimate(
            flops=flops,
            transcendentals=blocks * rows * seq // 2,
            bytes_accessed=2 * (q.size * 2 + k.size + v.size),
        ),
    )(x_index, q, k, v)


def shards(inner_gate, outer_gate, signal, filters, bypass, query_rows, key_rows):
    local_rows, channels = signal.shape
    nz = lax.axis_size("cz")
    nx = lax.axis_size("cx")
    members = nz * nx
    heads = channels // DH
    my_x = lax.axis_index("cx")

    product = (inner_gate.astype(jnp.float32) * signal.astype(jnp.float32)).astype(jnp.bfloat16)
    left_rim = lax.ppermute(
        product[local_rows - (TAPS - 1) :],
        ("cz", "cx"),
        [(i, i + 1) for i in range(members - 1)],
    )
    extended = jnp.concatenate([left_rim, product], axis=0)
    group_count = filters.shape[0]
    group_width = channels // group_count
    window_rows = local_rows + TAPS - 1
    band_hi, band_lo = banded_halves(filters, window_rows)
    windows = extended.reshape(window_rows, group_count, group_width)
    convolved = jnp.einsum(
        "gtj,jgc->tgc", band_hi, windows, preferred_element_type=jnp.float32
    ) + jnp.einsum("gtj,jgc->tgc", band_lo, windows, preferred_element_type=jnp.float32)
    convolved = convolved.reshape(local_rows, channels)
    hyena_out = (
        outer_gate.astype(jnp.float32) * (convolved + bypass[None, :] * product.astype(jnp.float32))
    ).astype(jnp.bfloat16)

    def by_head(a):
        return a.reshape(local_rows, heads, DH).transpose(1, 0, 2)

    stacked = jnp.stack([by_head(query_rows), by_head(key_rows), by_head(hyena_out)])
    spread = lax.all_to_all(stacked, "cz", 1, 1, tiled=True)
    q_here = spread[0]
    kv = lax.all_gather(spread[1:], "cx", axis=2, tiled=False)
    kv = kv.reshape(2, members * local_rows, DH)
    x_index = jnp.reshape(my_x, (1,)).astype(jnp.int32)
    out_here = attend_local(x_index, q_here, kv[0], kv[1], nx)
    returned = lax.all_to_all(out_here, "cz", 0, 0, tiled=True)
    attended = returned.transpose(1, 0, 2).reshape(local_rows, channels)
    return (hyena_out, attended)


def ctx_split(mesh):
    devices = np.asarray(mesh.devices)
    row = devices[0]
    try:
        nx = len({d.coords[0] for d in row})
    except Exception:
        nx = 4
    if row.size % nx:
        nx = 1
    return Mesh(devices.reshape(devices.shape[0], row.size // nx, nx), ("dp", "cz", "cx"))


def solution(mesh):
    split = ctx_split(mesh)
    rows = P(("dp", "cz", "cx"), None)
    placed = (rows, rows, rows, P(), P(), rows, rows)
    return jax.shard_map(
        shards,
        mesh=split,
        in_specs=placed,
        out_specs=(rows, rows),
        check_vma=False,
    )
```

time: 634 us -> 164 us (0.26)
  waiting for transfers between devices: 432 us -> 42.3 us
  starting transfers between devices: 77.6 us -> 10.8 us
  matrix products: 32.3 us -> 4.72 us
  loops' own time: 23.1 us -> 0 us
  local copies, waits for them, and re-layouts: 35 us -> 50.6 us
  blocking collectives: 18.1 us -> 32.9 us
  between operations: 1.46 us -> 14.2 us
  other arithmetic: 13 us -> 0.64 us
  Pallas kernels: 0 us -> 6.84 us
    ppermute x32 -> x1, waiting for transfers between devices: 432 us -> 0.01 us  [shards(): lax.ppermute(product[local_rows - (TAPS - 1):], ('cz', 'cx'), [(i, i + 1)...]
    ppermute x32 -> x1, starting transfers between devices: 64.7 us -> 3.41 us  [shards(): lax.ppermute(product[local_rows - (TAPS - 1):], ('cz', 'cx'), [(i, i + 1)...]
    all_gather x0 -> x1, waiting for transfers between devices: none -> 31.5 us  [shards(): kv = lax.all_gather(spread[1:], 'cx', axis=2, tiled=False)]
    dot_general x65 -> x2, matrix products: 32.3 us -> 4.72 us  [the longest x1 3.51 us: shards(): jnp.einsum('gtj,jgc->tgc', band_lo, windows, preferred_element_type=jnp.f...]
    another operation x33 -> x0, loops' own time: 23.1 us -> none  [the longest x1 21.4 us: attend(): lax.fori_loop(0, members - 1, chain_step, (first_state, stacked))]
    all_to_all x1, blocking collectives: 18.1 us -> 32.9 us  [shards(): spread = lax.all_to_all(stacked, 'cz', 1, 1, tiled=True)]
    reshape x3 -> x2, local copies, waits for them, and re-layouts: 18 us -> 31.8 us  [band(): jnp.tile(half, (1, taps))[:, :taps * window_rows]]
    all_to_all x1, waiting for transfers between devices: 0.01 us -> 10.9 us  [shards(): returned = lax.all_to_all(out_here, 'cz', 0, 0, tiled=True)]
  transfers between devices with their start and end apart: 33 -> 3, of which waited for: 31 -> 2; matrix products, arithmetic and copies ran while one was open for 6% -> 27% of each run, Pallas kernels for 0% -> 0%
where the time goes in v1:
time: 164 us; the launch traced here: 163 us
  local copies, waits for them, and re-layouts  50.6 us (31%)
  waiting for transfers between devices  42.3 us (26%)
  blocking collectives  32.9 us (20%)
  between operations  14.2 us (9%)
  starting transfers between devices  10.8 us (7%)
  Pallas kernels  6.84 us (4%)
  matrix products  4.72 us (3%)
    all_to_all x1, blocking collectives, shards(): spread = lax.all_to_all(stacked, 'cz', 1, 1, tiled=True)  32.9 us
    reshape x2, local copies, waits for them, and re-layouts, band(): jnp.tile(half, (1, taps))[:, :taps * window_rows]  31.8 us
    all_gather x1, waiting for transfers between devices, shards(): kv = lax.all_gather(spread[1:], 'cx', axis=2, tiled=False)  31.5 us
    all_to_all x1, waiting for transfers between devices, shards(): returned = lax.all_to_all(out_here, 'cz', 0, 0, tiled=True)  10.9 us
    unnamed x19, local copies, waits for them, and re-layouts  9.68 us
    all_to_all x1, starting transfers between devices, shards(): returned = lax.all_to_all(out_here, 'cz', 0, 0, tiled=True)  7.38 us
    pallas_call x1, Pallas kernels, attend_local(): pl.pallas_call(lambda *refs: attend_kernel(*refs, nx=nx), out_shape=jax.S...  6.84 us
    slice x2, local copies, waits for them, and re-layouts, band(): jnp.tile(half, (1, taps))[:, :taps * window_rows]  4.47 us
  transfers between devices with their start and end apart: 3, of which 2 were waited for; matrix products, arithmetic and copies ran while one was open for 27% of the time, Pallas kernels for 0%

profile of v1, /device:TPU:56, one launch (start us, length us, event | category | flops | bytes accessed | tf_op | source)
XLA Modules:
  0.0 163.1 jit_solution(2170058694550330929)
XLA Ops:
  7.2 1.1 copy.23
  8.3 1.1 copy.24
  9.5 0.1 slice.32
  9.7 3.4 %collective-permute-start = (bf16[127,1024]{0,1:T(8,128)(2,1)S(1)}, bf16[127,1024]{0,1:T(8,128)(2,1)S(1)}, u32[]{:S(2)}, u32[]{:S(2)}) collective-permute-start(bf16[127,1024]{0,1:T(8,128)(2,1)S(1)} %slice.32), channel_id=1, source_target_pairs={{0,1},{1,2},{2,3},{3,4},{4,5},{5,6},{6,7},{7,8},{8,9},{9,10},{10,1... | collective-permute-start | bytes 780296 | tf_op jit(solution)/shard_map/ppermute | solution.py:84
  13.1 0.8 rev.3
  13.9 0.3 tile.20
  14.2 2.6 %copy.34 = bf16[8,8,128,256]{3,1,2,0:T(8,128)(2,1)S(1)} copy(bf16[8,8,128,256]{3,2,1,0:T(8,128)(2,1)S(1)} %bitcast.43) | data formatting | bytes 8388608
  16.8 2.2 %slice.34 = bf16[64,32640]{1,0:T(8,128)(2,1)} slice(bf16[64,32768]{1,0:T(8,128)(2,1)S(1)} %bitcast.45), slice={[0:64], [0:32640]} | slice | bytes 8355840 | tf_op jit(solution)/shard_map/slice | solution.py:23
  19.1 15.9 %reshape.47 = bf16[64,128,255]{2,1,0:T(8,128)(2,1)} reshape(bf16[64,32640]{1,0:T(8,128)(2,1)} %slice.34) | data formatting | bytes 8355840 | tf_op jit(solution)/shard_map/reshape | solution.py:23
  34.9 0.3 tile.8
  35.2 2.6 %copy.33 = bf16[8,8,128,256]{3,1,2,0:T(8,128)(2,1)S(1)} copy(bf16[8,8,128,256]{3,2,1,0:T(8,128)(2,1)S(1)} %bitcast.44) | data formatting | bytes 8388608
  37.8 2.2 %slice.33 = bf16[64,32640]{1,0:T(8,128)(2,1)} slice(bf16[64,32768]{1,0:T(8,128)(2,1)S(1)} %bitcast.46), slice={[0:64], [0:32640]} | slice | bytes 8355840 | tf_op jit(solution)/shard_map/slice | solution.py:23
  40.1 15.9 %reshape.46 = bf16[64,128,255]{2,1,0:T(8,128)(2,1)} reshape(bf16[64,32640]{1,0:T(8,128)(2,1)} %slice.33) | data formatting | bytes 8355840 | tf_op jit(solution)/shard_map/reshape | solution.py:23
  56.0 0.2 copy.22
  56.2 0.2 copy.25
  56.4 0.2 copy.26
  56.6 0.2 pad_maximum_fusion.1
  56.8 3.5 %fusion.4 = f32[64,16,128]{2,1,0:T(8,128)S(1)} fusion(bf16[255,64,16]{0,2,1:T(8,128)(2,1)S(1)} %bitcast.47, bf16[64,128,255]{2,1,0:T(8,128)(2,1)} %reshape.47), kind=kOutput, calls=%fused_computation.12 | convolution fusion | flops 66846720 | bytes 5224448 | tf_op jit(solution)/shard_map/gtj,jgc->tgc/dot_general | solution.py:97
  60.3 1.2 convolution_add_fusion
  61.5 0.2 fusion.1
  61.8 0.1 pad_maximum_fusion
  61.9 0.4 copy.27
  62.3 32.9 %all_to_all.10 = bf16[3,8,128,128]{3,2,0,1:T(8,128)(2,1)S(1)} all-to-all(bf16[3,8,128,128]{3,2,0,1:T(8,128)(2,1)S(1)} %copy.27), channel_id=1, replica_groups=mesh['dp'=16,'cz'=8,'cx'=4] {'cz'}, dimensions={1} | all-to-all | bytes 1572864 | tf_op jit(solution)/shard_map/all_to_all | solution.py:107
  95.2 0.8 slice.36
  96.1 31.5 %all-gather.3.cloned.1.call-done = bf16[2,8,512,128]{3,2,0,1:T(8,128)(2,1)} async-done(((bf16[2,8,128,128]{3,2,0,1:T(8,128)(2,1)}), bf16[2,8,512,128]{3,2,0,1:T(8,128)(2,1)}) %all-gather.3.cloned.1.call-update) | async-done | bytes 2097168 | tf_op jit(solution)/shard_map/all_gather | solution.py:109
  127.6 1.7 %fusion.3 = (bf16[1,8,512,128]{3,2,0,1:T(8,128)(2,1)S(1)}, bf16[1,8,512,128]{3,2,0,1:T(8,128)(2,1)S(1)}) fusion(bf16[2,8,512,128]{3,2,0,1:T(8,128)(2,1)} %all-gather.3.cloned.1.call-done), kind=kLoop, calls=%fused_computation.11 | loop fusion | bytes 4194304 | tf_op jit(solution)/shard_map/slice | solution.py:112
  129.3 6.8 %shard_map.86 = bf16[8,128,128]{2,1,0:T(8,128)(2,1)} custom-call(s32[1]{0:T(128)} %bitcast.3.refs_0_, bf16[8,128,128]{2,1,0:T(8,128)(2,1)S(1)} %slice_bitcast_fusion.refs_1_, bf16[4096,128]{1,0:T(8,128)(2,1)S(1)} %bitcast.42, bf16[4096,128]{1,0:T(8,128)(2,1)S(1)} %bitcast.41), custom_call_target="tpu_custom_call" | custom-call | flops 1073741824 | bytes 2621440 | tf_op jit(solution)/shard_map/pallas_call | solution.py:56
  136.1 7.4 %all-to-all-start.1 = ((bf16[8,128,128]{2,1,0:T(8,128)(2,1)}), bf16[8,128,128]{2,1,0:T(8,128)(2,1)S(1)}, u32[]{:S(2)}, u32[]{:S(2)}) async-start(bf16[8,128,128]{2,1,0:T(8,128)(2,1)} %shard_map.86), calls=%async_computation.1 | async-start | bytes 524288 | tf_op jit(solution)/shard_map/all_to_all | solution.py:113
  143.5 0.8 copy.30
  144.4 10.9 %all-to-all-done.1 = bf16[8,128,128]{2,1,0:T(8,128)(2,1)S(1)} async-done(((bf16[8,128,128]{2,1,0:T(8,128)(2,1)}), bf16[8,128,128]{2,1,0:T(8,128)(2,1)S(1)}, u32[]{:S(2)}, u32[]{:S(2)}) %all-to-all-start.1) | async-done | bytes 262176 | tf_op jit(solution)/shard_map/all_to_all | solution.py:113
  155.2 0.2 copy.29
  155.4 0.9 copy.31
  (17 shorter events, 0.2 us)
Async XLA Ops:
  7.2 120.4 %all-gather.3.cloned.1.call-start = ((), (), s32[]{:S(2)}) async-start(), calls=%async_computation.2 | async-start | bytes 2621440 | tf_op jit(solution)/shard_map/all_gather | solution.py:109
  9.7 46.9 %collective-permute-start = (bf16[127,1024]{0,1:T(8,128)(2,1)S(1)}, bf16[127,1024]{0,1:T(8,128)(2,1)S(1)}, u32[]{:S(2)}, u32[]{:S(2)}) collective-permute-start(bf16[127,1024]{0,1:T(8,128)(2,1)S(1)} %slice.32), channel_id=1, source_target_pairs={{0,1},{1,2},{2,3},{3,4},{4,5},{5,6},{6,7},{7,8},{8,9},{9,10},{10,1... | collective-permute-start | bytes 780296 | tf_op jit(solution)/shard_map/ppermute | solution.py:84
  40.1 15.9 %copy-start.1 = (bf16[128,1024]{1,0:T(8,128)(2,1)S(1)}, bf16[128,1024]{1,0:T(8,128)(2,1)}, u32[]{:S(2)}) copy-start(bf16[128,1024]{1,0:T(8,128)(2,1)} %param.8) | copy-start | bytes 786436
  40.1 16.1 %copy-start.2 = (bf16[128,1024]{1,0:T(8,128)(2,1)S(1)}, bf16[128,1024]{1,0:T(8,128)(2,1)}, u32[]{:S(2)}) copy-start(bf16[128,1024]{1,0:T(8,128)(2,1)} %param.12) | copy-start | bytes 786436
  40.1 16.3 %copy-start.3 = (bf16[128,1024]{1,0:T(8,128)(2,1)S(1)}, bf16[128,1024]{1,0:T(8,128)(2,1)}, u32[]{:S(2)}) copy-start(bf16[128,1024]{1,0:T(8,128)(2,1)} %param.13) | copy-start | bytes 786436
  56.6 3.8 %copy-start = (bf16[64,128,255]{2,1,0:T(8,128)(2,1)S(1)}, bf16[64,128,255]{2,1,0:T(8,128)(2,1)}, u32[]{:S(2)}) copy-start(bf16[64,128,255]{2,1,0:T(8,128)(2,1)} %reshape.46) | copy-start | bytes 12533764
  60.3 1.2 copy-start.4
  136.1 19.1 %all-to-all-start.1 = ((bf16[8,128,128]{2,1,0:T(8,128)(2,1)}), bf16[8,128,128]{2,1,0:T(8,128)(2,1)S(1)}, u32[]{:S(2)}, u32[]{:S(2)}) async-start(bf16[8,128,128]{2,1,0:T(8,128)(2,1)} %shard_map.86), calls=%async_computation.1 | async-start | bytes 524288 | tf_op jit(solution)/shard_map/all_to_all | solution.py:113
Sparse Core Ops, SparseCore 0:
  96.2 31.3 all-gather.2
